TPU v7x, 256 devices: a whole 4x4x8 slice. The times are simulated.
256 devices in a mesh: dp: 2 (over y_hi), retr: 16 (over x, y_lo, core), tensor: 8 (over z).
Axes of the slice: x: 4, y: 4 (y_hi: 2, y_lo: 2; y = y_hi * 2 + y_lo), z: 8, core: 2. Of those that a mesh axis runs over, the one named last changes fastest.
Arguments:
- hidden_in: bfloat16 [16384, 4096], P(('dp', 'retr'), 'tensor'), may hold values from -12 to 12
- norm_gain: float32 [4096], replicated, may hold values from 0.1 to 1.9
- nbr_table: int32 [256, 2], P(('dp', 'retr')), may hold values from 0 to 63, as said below
- encodings: bfloat16 [64, 128, 1024], P('retr'), may hold values from -21 to 21
- enc_mask: int32 [64, 4], P('retr'), may hold values from 0 to 1, as said below
- w_query: bfloat16 [4096, 4096], P(None, 'tensor'), may hold values from -0.02703125 to 0.02703125
- w_key: bfloat16 [1024, 4096], P(None, 'tensor'), may hold values from -0.1021875 to 0.1021875
- w_value: bfloat16 [1024, 4096], P(None, 'tensor'), may hold values from -0.1875 to 0.1875
- w_out: bfloat16 [4096, 4096], P('tensor'), may hold values from -0.125 to 0.125
Outputs:
- mixed: bfloat16 [16384, 4096], P(('dp', 'retr'), 'tensor')
Inputs may be any that keep to these rules, and one draw needn't show every extreme that they name: `nbr_table`: each aligned block of 8 table rows (the rows of one device) holds 16 distinct ids; at most 2 of them share the value id // 4, and in every block some value of id // 4 has exactly 2. `enc_mask`: in each row the ones come first; the first entry is 1.
All inputs are finite; a program needn't handle non-finite values.
Results may differ from a plain program's by a relative error of at most 0.012.
The roundings to bfloat16 on the way count: a program that leaves them out, or rounds other values in their place, can miss the bound.
Values may be sent and summed in bfloat16 or wider, within the bound.
No kernel may reach another device: no remote copies, remote signals or barrier semaphores. Data moves between devices by JAX's collectives and lax.ppermute only.
A program may use at most 128 MiB of HBM per device.

v0:
```python
import math
import jax
import jax.numpy as jnp
from jax import lax
from jax.sharding import PartitionSpec as P

HD = 128
NBRS = 2
BLOCK = 32
CAP = 2


def attend_gathered(queries, key_value, selected_marks, segment_count, head_cols):
    tok_rows = queries.shape[0]
    head_count = head_cols // HD
    entry_keys = key_value.shape[0] // segment_count * key_value.shape[1]
    mask_cols = selected_marks.shape[1]
    key_block = key_value[:, :, :head_cols].reshape(segment_count, entry_keys, head_count, HD)
    value_block = key_value[:, :, head_cols:].reshape(segment_count, entry_keys, head_count, HD)
    key_live = (
        jnp.repeat(selected_marks.reshape(segment_count, NBRS * mask_cols), BLOCK, axis=1) > 0
    )
    query_block = queries.reshape(segment_count, tok_rows // segment_count, head_count, HD)
    factor = 1.0 / math.sqrt(HD)
    scores = (
        jnp.einsum("cqhd,ckhd->chqk", query_block, key_block, preferred_element_type=jnp.float32)
        * factor
    )
    key_open = key_live[:, None, None, :]
    scores = jnp.where(key_open, scores, -1e30)
    row_max = jnp.max(scores, axis=-1, keepdims=True)
    weights = jnp.exp(scores - row_max) * key_open.astype(jnp.float32)
    probabilities = (weights / jnp.sum(weights, axis=-1, keepdims=True)).astype(jnp.bfloat16)
    attended = jnp.einsum(
        "chqk,ckhd->cqhd", probabilities, value_block, preferred_element_type=jnp.float32
    )
    return attended.astype(jnp.bfloat16).reshape(tok_rows, head_cols)


def local(hidden_in, norm_gain, nbr_table, encodings, enc_mask, w_query, w_key, w_value, w_out):
    segment_count = nbr_table.shape[0]
    nb_dev, entry_len, enc_width = encodings.shape
    mask_cols = enc_mask.shape[1]
    head_cols = w_key.shape[1]
    wanted = nbr_table.reshape(-1)
    need_count = wanted.shape[0]
    info = jnp.concatenate([wanted, enc_mask.reshape(-1)])
    all_info = lax.all_gather(info, "retr", axis=0, tiled=False)
    retr_count = all_info.shape[0]
    all_wanted = all_info[:, :need_count]
    all_marks = all_info[:, need_count:].reshape(retr_count * nb_dev, mask_cols)
    gathered = lax.all_gather(hidden_in, "tensor", axis=1, tiled=True)
    w_both = jnp.concatenate([w_key, w_value], axis=1)
    own_kv = (
        jnp.dot(
            encodings.reshape(nb_dev * entry_len, enc_width),
            w_both,
            preferred_element_type=jnp.float32,
        )
        .astype(jnp.bfloat16)
        .reshape(nb_dev, entry_len * 2 * head_cols)
    )
    me = lax.axis_index("retr")
    mine = all_wanted // nb_dev == me
    rank = jnp.cumsum(mine.astype(jnp.int32), axis=1) - 1
    slot_ids = jnp.arange(CAP, dtype=jnp.int32)
    chosen = mine[:, None, :] & (rank[:, None, :] == slot_ids[None, :, None])
    local_idx = jnp.sum(jnp.where(chosen, all_wanted[:, None, :] % nb_dev, 0), axis=2)
    pick = (local_idx[:, :, None] == jnp.arange(nb_dev, dtype=jnp.int32)).astype(jnp.bfloat16)
    send = jnp.einsum("qjn,nf->qjf", pick, own_kv, preferred_element_type=jnp.float32).astype(
        jnp.bfloat16
    )
    recv = lax.all_to_all(send, "retr", 0, 0, tiled=True)
    owner = wanted // nb_dev
    same = owner[:, None] == owner[None, :]
    earlier = jnp.arange(need_count)[None, :] < jnp.arange(need_count)[:, None]
    my_rank = jnp.sum((same & earlier).astype(jnp.int32), axis=1)
    flat_idx = owner * CAP + my_rank
    key_value = jnp.take(recv.reshape(retr_count * CAP, -1), flat_idx, axis=0)
    key_value = key_value.reshape(need_count, entry_len, 2 * head_cols)
    picked_marks = jnp.take(all_marks, wanted, axis=0)
    widened = gathered.astype(jnp.float32)
    mean_sq = jnp.mean(widened * widened, axis=-1, keepdims=True)
    normed = (widened * lax.rsqrt(mean_sq + 1e-05) * norm_gain).astype(jnp.bfloat16)
    queries = jnp.dot(normed, w_query, preferred_element_type=jnp.float32).astype(jnp.bfloat16)
    attended = attend_gathered(queries, key_value, picked_marks, segment_count, head_cols)
    partial_value = jnp.dot(attended, w_out, preferred_element_type=jnp.float32)
    summed = lax.psum_scatter(
        partial_value.astype(jnp.bfloat16), "tensor", scatter_dimension=1, tiled=True
    )
    return (hidden_in.astype(jnp.float32) + summed.astype(jnp.float32)).astype(jnp.bfloat16)


def solution(mesh):
    in_specs = (
        P(("dp", "retr"), "tensor"),
        P(),
        P(("dp", "retr"), None),
        P("retr", None, None),
        P("retr", None),
        P(None, "tensor"),
        P(None, "tensor"),
        P(None, "tensor"),
        P("tensor", None),
    )
    out_specs = P(("dp", "retr"), "tensor")
    return jax.shard_map(local, mesh=mesh, in_specs=in_specs, out_specs=out_specs, check_vma=False)
```

profile of v0, /device:TPU:1, one launch (start us, length us, event | category | flops | bytes accessed | tf_op | source)
XLA Modules:
  0.0 317.1 jit_solution(4664920492474158840)
XLA Ops:
  6.5 0.7 all-gather.3.cloned.1.call-update
  7.3 0.8 copy.37
  8.0 0.1 reshape.243
  8.1 0.8 reshape.244
  8.9 1.3 dynamic-slice
  10.8 0.2 add_dynamic-update-slice_fusion
  11.0 10.8 %all-reduce = s32[512]{0:T(512)S(1)} all-reduce(s32[512]{0:T(512)S(1)} %add_dynamic-update-slice_fusion), channel_id=2, replica_groups=mesh['dp'=2,'retr'=16,'tensor'=8] {'retr'}, use_global_device_ids=true, to_apply=%add | all-reduce | flops 512 | bytes 4096
  21.8 0.1 reshape.278
  21.9 2.8 fusion.20
  24.7 0.2 reduce_window_sum.11
  24.9 0.5 copy.38
  25.4 0.8 reshape.284
  26.2 0.1 fusion.54
  26.3 0.1 select_reduce_fusion
  26.4 3.0 convolution_convert_fusion
  29.4 16.4 %copy.39 = bf16[16,2,131072]{2,1,0:T(2,128)(2,1)} copy(bf16[16,2,131072]{2,0,1:T(8,128)(2,1)S(1)} %convolution_convert_fusion) | data formatting | bytes 16777216 | tf_op jit(solution)/shard_map/convert_element_type | solution.py:70
  45.7 7.8 %all-to-all-start = ((bf16[16,2,131072]{2,1,0:T(2,128)(2,1)}), bf16[16,2,131072]{2,1,0:T(2,128)(2,1)}, u32[]{:S(2)}, u32[]{:S(2)}) async-start(bf16[16,2,131072]{2,1,0:T(2,128)(2,1)} %copy.39), calls=%async_computation | async-start | bytes 16777216 | tf_op jit(solution)/shard_map/all_to_all | solution.py:73
  53.5 0.1 reshape.248
  53.7 0.2 convert_reduce_fusion
  53.9 0.6 gather_fusion
  54.5 0.1 gather.15
  54.6 0.1 copy.42
  54.7 0.1 copy.43
  54.8 0.1 broadcast_in_dim.71
  54.8 0.1 gt.19
  55.0 12.6 %all-gather.3.cloned.1.call-done = bf16[512,4096]{1,0:T(8,128)(2,1)} async-done(((bf16[512,512]{1,0:T(8,128)(2,1)}), bf16[512,4096]{1,0:T(8,128)(2,1)}) %all-gather.3.cloned.1.call-update) | async-done | bytes 4194320 | tf_op jit(solution)/shard_map/all_gather | solution.py:52
  67.5 3.2 %fusion.1 = f32[512]{0:T(512)S(1)} fusion(bf16[512,4096]{1,0:T(8,128)(2,1)} %all-gather.3.cloned.1.call-done), kind=kLoop, calls=%fused_computation.7 | loop fusion | flops 6290944 | bytes 4196352 | tf_op jit(solution)/shard_map/reduce_sum | solution.py:83
  70.8 0.2 copy-done.2
  71.0 4.6 %fusion.26 = bf16[512,512]{1,0:T(8,128)(2,1)S(1)} fusion(bf16[4096,512]{1,0:T(8,128)(2,1)} %param.14, bf16[512,4096]{1,0:T(8,128)(2,1)S(1)} %copy-done.2, f32[4096]{0:T(1024)S(1)} %copy-done.7, f32[512]{0:T(512)S(1)} %add_rsqrt_fusion), kind=kOutput, calls=%fused_computation.31 | convolution fusion | flops 2156134400 | bytes 8931328 | tf_op jit(solution)/shard_map/dot_general | solution.py:85
  75.6 0.1 reshape.251
  75.7 108.4 %all-to-all-done = bf16[16,2,131072]{2,1,0:T(2,128)(2,1)} async-done(((bf16[16,2,131072]{2,1,0:T(2,128)(2,1)}), bf16[16,2,131072]{2,1,0:T(2,128)(2,1)}, u32[]{:S(2)}, u32[]{:S(2)}) %all-to-all-start) | async-done | bytes 8388640 | tf_op jit(solution)/shard_map/all_to_all | solution.py:73
  184.0 8.4 %reshape.247 = bf16[32,131072]{1,0:T(8,128)(2,1)} reshape(bf16[16,2,131072]{2,1,0:T(2,128)(2,1)} %all-to-all-done) | data formatting | bytes 16777216 | tf_op jit(solution)/shard_map/reshape | solution.py:79
  192.5 5.7 %fusion.52 = (bf16[32,65536]{1,0:T(8,128)(2,1)}, bf16[32,65536]{1,0:T(8,128)(2,1)}) fusion(bf16[32,131072]{1,0:T(8,128)(2,1)} %reshape.247), kind=kLoop, calls=%fused_computation.86 | loop fusion | bytes 16777216 | tf_op jit(solution)/shard_map/jit(_take)/gather | solution.py:79
  198.2 6.4 %gather_fusion.1 = bf16[16,65536]{1,0:T(8,128)(2,1)S(1)} fusion(bf16[32,65536]{1,0:T(8,128)(2,1)} %get-tuple-element.8, s32[1024]{0:T(1024)S(1)} %get-tuple-element.19), kind=kCustom, calls=%fused_computation.1 | custom fusion | bytes 4194368 | tf_op jit(solution)/shard_map/jit(_take)/gather | solution.py:79
  204.5 7.7 %gather_fusion.2 = bf16[16,65536]{1,0:T(8,128)(2,1)} fusion(bf16[32,65536]{1,0:T(8,128)(2,1)} %get-tuple-element.9, s32[1024]{0:T(1024)S(1)} %get-tuple-element.19), kind=kCustom, calls=%fused_computation.2 | custom fusion | bytes 4194368 | tf_op jit(solution)/shard_map/jit(_take)/gather | solution.py:79
  212.2 1.9 pad_maximum_fusion
  214.1 4.2 %copy.48 = bf16[2,8,128,1024]{3,2,1,0:T(8,128)(2,1)} copy(bf16[2,8,128,1024]{3,1,2,0:T(8,128)(2,1)S(1)} %bitcast.31) | data formatting | bytes 8388608
  218.3 6.9 %copy.41 = bf16[16,128,1024]{1,0,2:T(8,128)(2,1)} copy(bf16[16,128,1024]{2,1,0:T(8,128)(2,1)} %bitcast.32) | data formatting | bytes 8388608 | tf_op jit(solution)/shard_map/jit(_take)/gather | solution.py:79
  225.2 2.6 broadcast_select_fusion
  227.9 2.0 fusion.53
  229.9 4.1 %reshape.252 = bf16[8,256,4,128]{1,0,3,2:T(8,128)(2,1)} reshape(bf16[16,128,512]{1,0,2:T(8,128)(2,1)} %get-tuple-element.10) | data formatting | bytes 4194304 | tf_op jit(solution)/shard_map/reshape | solution.py:18
  233.9 2.2 reshape.249
  236.1 4.4 %fusion.55 = (f32[8,4,64]{2,1,0:T(4,128)S(1)}, f32[8,4,64,256]{3,2,1,0:T(8,128)}) fusion(f32[8,256]{1,0:T(8,128)S(1)} %convert_element_type.63, pred[8,256]{1,0:T(8,128)(4,1)S(1)} %gt.19, bf16[8,256,4,128]{1,0,3,2:T(8,128)(2,1)} %reshape.252, bf16[8,64,4,128]{3,2,1,0:T(4,128)(2,1)S(1)} %reshape.251), kind=kOutput, calls=%fused_computation.89 | convolution fusion | flops 136839424 | bytes 4737024 | tf_op jit(solution)/shard_map/sub | solution.py:32
  240.5 2.6 fusion.29
  243.2 0.4 copy.47
  243.6 4.3 %convolution_convert_fusion.1 = bf16[512,4096]{1,0:T(8,128)(2,1)} fusion(bf16[512,4096]{1,0:T(8,128)(2,1)S(1)} %copy-done.6, bf16[64,8,4,128]{3,2,1,0:T(4,128)(2,1)S(1)} %bitcast.33), kind=kOutput, calls=%fused_computation.10 | convolution fusion | flops 2149580800 | bytes 8912896 | tf_op jit(solution)/shard_map/dot_general | solution.py:87
  247.9 60.3 %reduce-scatter.2.cloned.1.call-done = bf16[512,512]{1,0:T(8,128)(2,1)} async-done(((bf16[512,4096]{1,0:T(8,128)(2,1)}), bf16[512,512]{1,0:T(8,128)(2,1)}) %reduce-scatter.2.cloned.1.call-update) | async-done | bytes 524304 | tf_op jit(solution)/shard_map/reduce_scatter | solution.py:88
  308.2 2.0 add_convert_fusion
  (30 shorter events, 0.3 us)
Async XLA Ops:
  6.5 15.3 %copy-start = (bf16[4,128,1024]{2,1,0:T(8,128)(2,1)S(1)}, bf16[4,128,1024]{2,1,0:T(8,128)(2,1)}, u32[]{:S(2)}) copy-start(bf16[4,128,1024]{2,1,0:T(8,128)(2,1)} %param.12) | copy-start | bytes 3145732
  6.5 61.0 %all-gather.3.cloned.1.call-start = ((), (), s32[]{:S(2)}) async-start(), calls=%async_computation.2 | async-start | bytes 4718592 | tf_op jit(solution)/shard_map/all_gather | solution.py:52
  45.7 8.9 %copy-start.5 = (s32[8,2]{0,1:T(2,128)S(1)}, s32[8,2]{0,1:T(2,128)}, u32[]{:S(2)}) copy-start(s32[8,2]{0,1:T(2,128)} %param.11) | copy-start | bytes 196
  45.7 138.3 %all-to-all-start = ((bf16[16,2,131072]{2,1,0:T(2,128)(2,1)}), bf16[16,2,131072]{2,1,0:T(2,128)(2,1)}, u32[]{:S(2)}, u32[]{:S(2)}) async-start(bf16[16,2,131072]{2,1,0:T(2,128)(2,1)} %copy.39), calls=%async_computation | async-start | bytes 16777216 | tf_op jit(solution)/shard_map/all_to_all | solution.py:73
  53.5 17.3 %copy-start.7 = (f32[4096]{0:T(1024)S(1)}, f32[4096]{0:T(1024)}, u32[]{:S(2)}) copy-start(f32[4096]{0:T(1024)} %param.10) | copy-start | bytes 49156
  53.5 254.8 %reduce-scatter.2.cloned.1.call-start = ((), (), s32[]{:S(2)}) async-start(), calls=%async_computation.3 | async-start | bytes 4718592 | tf_op jit(solution)/shard_map/reduce_scatter | solution.py:88
  67.5 3.4 %copy-start.2 = (bf16[512,4096]{1,0:T(8,128)(2,1)S(1)}, bf16[512,4096]{1,0:T(8,128)(2,1)}, u32[]{:S(2)}) copy-start(bf16[512,4096]{1,0:T(8,128)(2,1)} %all-gather.3.cloned.1.call-done) | copy-start | bytes 12582916
  236.1 4.4 %copy-start.4 = (bf16[8,256,4,128]{1,0,3,2:T(8,128)(2,1)S(1)}, bf16[8,256,4,128]{1,0,3,2:T(8,128)(2,1)}, u32[]{:S(2)}) copy-start(bf16[8,256,4,128]{1,0,3,2:T(8,128)(2,1)} %reshape.249) | copy-start | bytes 6291460
  240.5 3.1 copy-start.6
  243.6 66.6 %copy-start.1 = (bf16[4,128,1024]{2,1,0:T(8,128)(2,1)S(1)}, bf16[4,128,1024]{2,1,0:T(8,128)(2,1)}, u32[]{:S(2)}) copy-start(bf16[4,128,1024]{2,1,0:T(8,128)(2,1)} %param.12) | copy-start | bytes 3145732
  247.9 60.4 %copy-start.3 = (bf16[512,512]{1,0:T(8,128)(2,1)S(1)}, bf16[512,512]{1,0:T(8,128)(2,1)}, u32[]{:S(2)}) copy-start(bf16[512,512]{1,0:T(8,128)(2,1)} %param.9) | copy-start | bytes 1572868
Sparse Core Ops, SparseCore 0:
  9.1 58.3 all-gather.2
  248.0 60.1 reduce-scatter.1
where the time goes:
time: 318 us; the launch traced here: 317 us
  waiting for transfers between devices  182 us (57%)
  local copies, waits for them, and re-layouts  70 us (22%)
  matrix products  21.7 us (7%)
  between operations  14.2 us (4%)
  blocking collectives  10.8 us (3%)
  other arithmetic  10.5 us (3%)
  starting transfers between devices  7.8 us (2%)
    all_to_all x1, waiting for transfers between devices, local(): recv = lax.all_to_all(send, 'retr', 0, 0, tiled=True)  108 us
    reduce_scatter x1, waiting for transfers between devices, local(): lax.psum_scatter(partial_value.astype(jnp.bfloat16), 'tensor', scatter_di...  60.3 us
    gather x4, local copies, waits for them, and re-layouts, local(): key_value = jnp.take(recv.reshape(retr_count * CAP, -1), flat_idx, axis=0)  26.6 us
    convert_element_type x1, local copies, waits for them, and re-layouts, local(): jnp.einsum('qjn,nf->qjf', pick, own_kv, preferred_element_type=jnp.float32)  16.4 us
    all_gather x1, waiting for transfers between devices, local(): gathered = lax.all_gather(hidden_in, 'tensor', axis=1, tiled=True)  12.6 us
    unnamed x1, blocking collectives  10.8 us
    reshape x1, local copies, waits for them, and re-layouts, local(): key_value = jnp.take(recv.reshape(retr_count * CAP, -1), flat_idx, axis=0)  8.44 us
    all_to_all x1, starting transfers between devices, local(): recv = lax.all_to_all(send, 'retr', 0, 0, tiled=True)  7.76 us
  transfers between devices with their start and end apart: 3, of which 3 were waited for; matrix products, arithmetic and copies ran while one was open for 11% of the time, Pallas kernels for 0%

commit v1 on v0

--- a/solution.py
+++ b/solution.py
@@ -49,7 +49,9 @@
     retr_count = all_info.shape[0]
     all_wanted = all_info[:, :need_count]
     all_marks = all_info[:, need_count:].reshape(retr_count * nb_dev, mask_cols)
-    gathered = lax.all_gather(hidden_in, "tensor", axis=1, tiled=True)
+    gathered = jnp.concatenate(
+        lax.all_to_all(jnp.stack([hidden_in] * lax.axis_size("tensor")), "tensor", 0, 0), axis=1
+    )
     w_both = jnp.concatenate([w_key, w_value], axis=1)
     own_kv = (
         jnp.dot(

time: 318 us -> 379 us (1.19)
  waiting for transfers between devices: 182 us -> 233 us
  starting transfers between devices: 7.8 us -> 15 us
    all_to_all x0 -> x1, waiting for transfers between devices: none -> 59.7 us  [local(): lax.all_to_all(jnp.stack([hidden_in] * lax.axis_size('tensor')), 'tensor'...]
    all_to_all x1, waiting for transfers between devices: 108 us -> 121 us  [local(): recv = lax.all_to_all(send, 'retr', 0, 0, tiled=True)]
    all_gather x1 -> x0, waiting for transfers between devices: 12.6 us -> none  [local(): gathered = lax.all_gather(hidden_in, 'tensor', axis=1, tiled=True)]
    all_to_all x0 -> x1, starting transfers between devices: none -> 9.13 us  [local(): lax.all_to_all(jnp.stack([hidden_in] * lax.axis_size('tensor')), 'tensor'...]
    reduce_scatter x1, waiting for transfers between devices: 60.3 us -> 52.3 us  [local(): lax.psum_scatter(partial_value.astype(jnp.bfloat16), 'tensor', scatter_di...]
  transfers between devices with their start and end apart: 3 -> 3, of which waited for: 3 -> 3; matrix products, arithmetic and copies ran while one was open for 11% -> 9% of each run, Pallas kernels for 0% -> 0%
where the time goes in v1:
time: 379 us
  waiting for transfers between devices  233 us (61%)
  local copies, waits for them, and re-layouts  72 us (19%)
  matrix products  19.5 us (5%)
  starting transfers between devices  15 us (4%)
  between operations  14.2 us (4%)
  other arithmetic  13.3 us (4%)
  blocking collectives  11.5 us (3%)
    all_to_all x1, waiting for transfers between devices, local(): recv = lax.all_to_all(send, 'retr', 0, 0, tiled=True)  121 us
    all_to_all x1, waiting for transfers between devices, local(): lax.all_to_all(jnp.stack([hidden_in] * lax.axis_size('tensor')), 'tensor'...  59.7 us
    reduce_scatter x1, waiting for transfers between devices, local(): lax.psum_scatter(partial_value.astype(jnp.bfloat16), 'tensor', scatter_di...  52.3 us
    gather x4, local copies, waits for them, and re-layouts, local(): key_value = jnp.take(recv.reshape(retr_count * CAP, -1), flat_idx, axis=0)  26.6 us
    convert_element_type x1, local copies, waits for them, and re-layouts, local(): jnp.einsum('qjn,nf->qjf', pick, own_kv, preferred_element_type=jnp.float32)  16.4 us
    unnamed x1, blocking collectives  11.5 us
    all_to_all x1, starting transfers between devices, local(): lax.all_to_all(jnp.stack([hidden_in] * lax.axis_size('tensor')), 'tensor'...  9.13 us
    reshape x1, local copies, waits for them, and re-layouts, local(): key_value = jnp.take(recv.reshape(retr_count * CAP, -1), flat_idx, axis=0)  8.43 us
  transfers between devices with their start and end apart: 3, of which 3 were waited for; matrix products, arithmetic and copies ran while one was open for 9% of the time, Pallas kernels for 0%

profile of v1, /device:TPU:1, one launch (start us, length us, event | category | flops | bytes accessed | tf_op | source)
XLA Modules:
  0.0 378.5 jit_solution(1549500198755615997)
XLA Ops:
  6.5 1.3 copy.46
  7.9 2.3 stack.2
  10.2 9.1 %all-to-all-start.1 = ((bf16[8,512,512]{1,2,0:T(8,128)(2,1)}), bf16[8,512,512]{1,2,0:T(8,128)(2,1)}, u32[]{:S(2)}, u32[]{:S(2)}) async-start(bf16[8,512,512]{1,2,0:T(8,128)(2,1)} %stack.2), calls=%async_computation.1 | async-start | bytes 8388608 | tf_op jit(solution)/shard_map/all_to_all | solution.py:53
  19.3 0.1 copy.39
  19.4 0.1 reshape.249
  19.5 0.1 reshape.250
  19.6 0.6 dynamic-slice
  20.8 0.2 add_dynamic-update-slice_fusion
  21.0 11.5 %all-reduce = s32[512]{0:T(512)S(1)} all-reduce(s32[512]{0:T(512)S(1)} %add_dynamic-update-slice_fusion), channel_id=2, replica_groups=mesh['dp'=2,'retr'=16,'tensor'=8] {'retr'}, use_global_device_ids=true, to_apply=%add | all-reduce | flops 512 | bytes 4096
  32.5 0.1 reshape.285
  32.6 0.2 reduce_window_sum.11
  32.7 2.8 fusion.15
  35.6 0.5 copy.40
  36.1 0.8 reshape.291
  37.0 0.1 select_reduce_fusion
  37.1 3.0 convolution_convert_fusion
  40.1 16.4 %copy.41 = bf16[16,2,131072]{2,1,0:T(2,128)(2,1)} copy(bf16[16,2,131072]{2,0,1:T(8,128)(2,1)S(1)} %convolution_convert_fusion) | data formatting | bytes 16777216 | tf_op jit(solution)/shard_map/convert_element_type | solution.py:72
  56.4 59.7 %all-to-all-done.1 = bf16[8,512,512]{1,2,0:T(8,128)(2,1)} async-done(((bf16[8,512,512]{1,2,0:T(8,128)(2,1)}), bf16[8,512,512]{1,2,0:T(8,128)(2,1)}, u32[]{:S(2)}, u32[]{:S(2)}) %all-to-all-start.1) | async-done | bytes 4194336 | tf_op jit(solution)/shard_map/all_to_all | solution.py:53
  116.2 5.8 %all-to-all-start = ((bf16[16,2,131072]{2,1,0:T(2,128)(2,1)}), bf16[16,2,131072]{2,1,0:T(2,128)(2,1)}, u32[]{:S(2)}, u32[]{:S(2)}) async-start(bf16[16,2,131072]{2,1,0:T(2,128)(2,1)} %copy.41), calls=%async_computation | async-start | bytes 16777216 | tf_op jit(solution)/shard_map/all_to_all | solution.py:75
  122.0 0.1 reshape.254
  122.2 0.2 convert_reduce_fusion
  122.4 0.6 gather_fusion
  123.2 0.1 copy.45
  123.3 0.1 broadcast_in_dim.71
  123.3 0.1 gt.19
  123.5 3.1 multiply_reduce_fusion
  126.6 2.9 fusion.2
  129.6 0.5 copy-done.7
  130.1 2.3 convolution_convert_fusion.2
  132.4 0.1 reshape.257
  132.5 121.0 %all-to-all-done = bf16[16,2,131072]{2,1,0:T(2,128)(2,1)} async-done(((bf16[16,2,131072]{2,1,0:T(2,128)(2,1)}), bf16[16,2,131072]{2,1,0:T(2,128)(2,1)}, u32[]{:S(2)}, u32[]{:S(2)}) %all-to-all-start) | async-done | bytes 8388640 | tf_op jit(solution)/shard_map/all_to_all | solution.py:75
  253.5 8.4 %reshape.253 = bf16[32,131072]{1,0:T(8,128)(2,1)} reshape(bf16[16,2,131072]{2,1,0:T(2,128)(2,1)} %all-to-all-done) | data formatting | bytes 16777216 | tf_op jit(solution)/shard_map/reshape | solution.py:81
  262.0 5.7 %fusion.44 = (bf16[32,65536]{1,0:T(8,128)(2,1)}, bf16[32,65536]{1,0:T(8,128)(2,1)}) fusion(bf16[32,131072]{1,0:T(8,128)(2,1)} %reshape.253), kind=kLoop, calls=%fused_computation.82 | loop fusion | bytes 16777216 | tf_op jit(solution)/shard_map/jit(_take)/gather | solution.py:81
  267.6 6.4 %gather_fusion.1 = bf16[16,65536]{1,0:T(8,128)(2,1)S(1)} fusion(bf16[32,65536]{1,0:T(8,128)(2,1)} %get-tuple-element.8, s32[1024]{0:T(1024)S(1)} %get-tuple-element.19), kind=kCustom, calls=%fused_computation.1 | custom fusion | bytes 4194368 | tf_op jit(solution)/shard_map/jit(_take)/gather | solution.py:81
  274.0 7.7 %gather_fusion.2 = bf16[16,65536]{1,0:T(8,128)(2,1)} fusion(bf16[32,65536]{1,0:T(8,128)(2,1)} %get-tuple-element.9, s32[1024]{0:T(1024)S(1)} %get-tuple-element.19), kind=kCustom, calls=%fused_computation.2 | custom fusion | bytes 4194368 | tf_op jit(solution)/shard_map/jit(_take)/gather | solution.py:81
  281.7 1.9 pad_maximum_fusion
  283.6 4.3 %copy.51 = bf16[2,8,128,1024]{3,2,1,0:T(8,128)(2,1)} copy(bf16[2,8,128,1024]{3,1,2,0:T(8,128)(2,1)S(1)} %bitcast.40) | data formatting | bytes 8388608
  287.8 6.9 %copy.43 = bf16[16,128,1024]{1,0,2:T(8,128)(2,1)} copy(bf16[16,128,1024]{2,1,0:T(8,128)(2,1)} %bitcast.41) | data formatting | bytes 8388608 | tf_op jit(solution)/shard_map/jit(_take)/gather | solution.py:81
  294.7 2.6 broadcast_select_fusion
  297.4 2.0 fusion.45
  299.4 4.1 %reshape.258 = bf16[8,256,4,128]{1,0,3,2:T(8,128)(2,1)} reshape(bf16[16,128,512]{1,0,2:T(8,128)(2,1)} %get-tuple-element.10) | data formatting | bytes 4194304 | tf_op jit(solution)/shard_map/reshape | solution.py:18
  303.4 2.2 reshape.255
  305.6 4.4 %fusion.47 = (f32[8,4,64]{2,1,0:T(4,128)S(1)}, f32[8,4,64,256]{3,2,1,0:T(8,128)}) fusion(f32[8,256]{1,0:T(8,128)S(1)} %convert_element_type.76, pred[8,256]{1,0:T(8,128)(4,1)S(1)} %gt.19, bf16[8,256,4,128]{1,0,3,2:T(8,128)(2,1)} %reshape.258, bf16[8,64,4,128]{3,2,1,0:T(4,128)(2,1)S(1)} %reshape.257), kind=kOutput, calls=%fused_computation.85 | convolution fusion | flops 136839424 | bytes 4737024 | tf_op jit(solution)/shard_map/sub | solution.py:32
  310.0 2.6 fusion.21
  312.7 0.4 copy.50
  313.1 4.3 %convolution_convert_fusion.1 = bf16[512,4096]{1,0:T(8,128)(2,1)} fusion(bf16[512,4096]{1,0:T(8,128)(2,1)S(1)} %copy-done.8, bf16[64,8,4,128]{3,2,1,0:T(4,128)(2,1)S(1)} %bitcast.42), kind=kOutput, calls=%fused_computation.9 | convolution fusion | flops 2149580800 | bytes 8912896 | tf_op jit(solution)/shard_map/dot_general | solution.py:89
  317.4 52.3 %reduce-scatter.2.cloned.1.call-done = bf16[512,512]{1,0:T(8,128)(2,1)} async-done(((bf16[512,4096]{1,0:T(8,128)(2,1)}), bf16[512,512]{1,0:T(8,128)(2,1)}) %reduce-scatter.2.cloned.1.call-update) | async-done | bytes 524304 | tf_op jit(solution)/shard_map/reduce_scatter | solution.py:90
  369.7 2.0 add_convert_fusion
  (36 shorter events, 0.5 us)
Async XLA Ops:
  6.5 26.2 %copy-start = (bf16[4,128,1024]{2,1,0:T(8,128)(2,1)S(1)}, bf16[4,128,1024]{2,1,0:T(8,128)(2,1)}, u32[]{:S(2)}) copy-start(bf16[4,128,1024]{2,1,0:T(8,128)(2,1)} %param.12) | copy-start | bytes 3145732
  10.2 9.1 %copy-start.6 = (s32[8,2]{0,1:T(2,128)S(1)}, s32[8,2]{0,1:T(2,128)}, u32[]{:S(2)}) copy-start(s32[8,2]{0,1:T(2,128)} %param.11) | copy-start | bytes 196
  10.2 9.3 %copy-start.5 = (s32[4,4]{1,0:T(4,128)S(1)}, s32[4,4]{1,0:T(4,128)}, u32[]{:S(2)}) copy-start(s32[4,4]{1,0:T(4,128)} %param.13) | copy-start | bytes 196
  10.2 9.4 %copy-start.9 = (u32[256]{0:T(256)S(1)}, u32[256]{0:T(256)}, u32[]{:S(2)}) copy-start(u32[256]{0:T(256)} %constant.99) | copy-start | bytes 3076
  10.2 106.0 %all-to-all-start.1 = ((bf16[8,512,512]{1,2,0:T(8,128)(2,1)}), bf16[8,512,512]{1,2,0:T(8,128)(2,1)}, u32[]{:S(2)}, u32[]{:S(2)}) async-start(bf16[8,512,512]{1,2,0:T(8,128)(2,1)} %stack.2), calls=%async_computation.1 | async-start | bytes 8388608 | tf_op jit(solution)/shard_map/all_to_all | solution.py:53
  116.2 137.4 %all-to-all-start = ((bf16[16,2,131072]{2,1,0:T(2,128)(2,1)}), bf16[16,2,131072]{2,1,0:T(2,128)(2,1)}, u32[]{:S(2)}, u32[]{:S(2)}) async-start(bf16[16,2,131072]{2,1,0:T(2,128)(2,1)} %copy.41), calls=%async_computation | async-start | bytes 16777216 | tf_op jit(solution)/shard_map/all_to_all | solution.py:75
  122.0 4.6 %copy-start.4 = (f32[4096]{0:T(1024)S(1)}, f32[4096]{0:T(1024)}, u32[]{:S(2)}) copy-start(f32[4096]{0:T(1024)} %param.10) | copy-start | bytes 49156
  122.0 247.7 %reduce-scatter.2.cloned.1.call-start = ((), (), s32[]{:S(2)}) async-start(), calls=%async_computation.3 | async-start | bytes 4718592 | tf_op jit(solution)/shard_map/reduce_scatter | solution.py:90
  126.6 3.5 copy-start.7
  305.6 4.4 %copy-start.3 = (bf16[8,256,4,128]{1,0,3,2:T(8,128)(2,1)S(1)}, bf16[8,256,4,128]{1,0,3,2:T(8,128)(2,1)}, u32[]{:S(2)}) copy-start(bf16[8,256,4,128]{1,0,3,2:T(8,128)(2,1)} %reshape.255) | copy-start | bytes 6291460
  310.0 3.1 copy-start.8
  313.1 58.6 %copy-start.1 = (bf16[4,128,1024]{2,1,0:T(8,128)(2,1)S(1)}, bf16[4,128,1024]{2,1,0:T(8,128)(2,1)}, u32[]{:S(2)}) copy-start(bf16[4,128,1024]{2,1,0:T(8,128)(2,1)} %param.12) | copy-start | bytes 3145732
  317.4 52.3 %copy-start.2 = (bf16[512,512]{1,0:T(8,128)(2,1)S(1)}, bf16[512,512]{1,0:T(8,128)(2,1)}, u32[]{:S(2)}) copy-start(bf16[512,512]{1,0:T(8,128)(2,1)} %param.9) | copy-start | bytes 1572868
Sparse Core Ops, SparseCore 0:
  317.5 52.1 reduce-scatter.1
